TPU v7x, 512 devices: a whole 4x8x8 slice. The times are simulated.
512 devices in a mesh: row: 32 (over z, x), col: 16 (over y, core).
Axes of the slice: x: 4, y: 8, z: 8, core: 2. Of those that a mesh axis runs over, the one named last changes fastest.
Arguments:
- tokens: bfloat16 [16384, 5376], P('row', 'col'), may hold values from -240 to 240
- gain: float32 [5376], P('col'), may hold values from 0.1 to 1.9
- query_gain: float32 [128], replicated, may hold values from 0.1 to 1.9
- key_gain: float32 [128], replicated, may hold values from 0.1 to 1.9
- w_query: bfloat16 [5376, 4096], P('row', 'col'), may hold values from -0.21808224 to 0.21808224
- w_key: bfloat16 [5376, 2048], P('row', 'col'), may hold values from -0.21808224 to 0.21808224
- w_value: bfloat16 [5376, 2048], P('row', 'col'), may hold values from -0.21808224 to 0.21808224
Outputs:
- attended: bfloat16 [16384, 4096], P('row', 'col')
All inputs are finite; a program needn't handle non-finite values.
Results may differ from a plain program's by a relative error of at most 0.022.
Values may be sent and summed in bfloat16 or wider, within the bound.
No kernel may reach another device: no remote copies, remote signals or barrier semaphores. Data moves between devices by JAX's collectives and lax.ppermute only.
A program may use at most 64 MiB of HBM per device.

v0:
```python
import jax
import jax.numpy as jnp
from jax import lax
from jax.sharding import Mesh, PartitionSpec as P

D = 5376
HD = 128
WINDOW = 1024
EPS = 1e-06
CLIP_FRACTION = 0.25
QUERY_SCALAR = 168.0
ROPE_BASE = 10000.0
ROW = ("rz", "rx")


def shifted(array, axis, by):
    peers = lax.axis_size(axis)
    pairs = [(i, i + by) for i in range(peers) if 0 <= i + by < peers]
    return lax.ppermute(array, axis, pairs)


def ring_gather(parts, axis, dims):
    peers = lax.axis_size(axis)
    right = [(i, (i + 1) % peers) for i in range(peers)]
    left = [(i, (i - 1) % peers) for i in range(peers)]
    held = {0: parts}
    forward = parts
    backward = parts
    for step in range(1, peers // 2 + 1):
        forward = lax.ppermute(forward, axis, right)
        held[peers - step] = forward
        if step < peers - step:
            backward = lax.ppermute(backward, axis, left)
            held[step] = backward
    start = (peers - lax.axis_index(axis)) % peers
    out = []
    for leaf, dim in enumerate(dims):
        stacked = jnp.concatenate([held[k][leaf] for k in range(peers)], axis=dim)
        doubled = jnp.concatenate([stacked, stacked], axis=dim)
        size = parts[leaf].shape[dim]
        out.append(lax.dynamic_slice_in_dim(doubled, start * size, peers * size, dim))
    return tuple(out)


def clip_with(weight, largest):
    bound = CLIP_FRACTION * largest
    return jnp.clip(weight.astype(jnp.float32), -bound, bound).astype(jnp.bfloat16)


def column_max(weight):
    return jnp.max(jnp.abs(weight.astype(jnp.float32)), axis=0)


def head_norm(values, head_gain):
    return values * lax.rsqrt(jnp.mean(values * values, axis=-1, keepdims=True) + EPS) * head_gain


def rotate(values, positions):
    half = values.shape[-1] // 2
    freqs = ROPE_BASE ** (-(jnp.arange(half, dtype=jnp.float32) * 2.0 / values.shape[-1]))
    angles = positions.astype(jnp.float32)[:, None] * freqs[None, :]
    cosine = jnp.cos(angles)[:, None, :]
    sine = jnp.sin(angles)[:, None, :]
    first = values[..., :half]
    second = values[..., half:]
    return jnp.concatenate(
        [first * cosine - second * sine, second * cosine + first * sine], axis=-1
    )


def local(tokens, gain, query_gain, key_gain, w_query, w_key, w_value):
    rows = tokens.shape[0]
    query_cols = w_query.shape[1]
    key_cols = w_key.shape[1]
    stacked = jnp.concatenate([w_query, w_key, w_value], axis=1)
    weight_rows, weight_cols = stacked.shape
    aligned = -(-(weight_rows + 1) // TILE_ROWS) * TILE_ROWS
    local_max = jnp.max(jnp.abs(stacked), axis=0)
    padded = jnp.concatenate(
        [
            stacked,
            local_max[None],
            jnp.zeros((aligned - weight_rows - 1, weight_cols), stacked.dtype),
        ],
        axis=0,
    )
    placed = jnp.zeros((lax.axis_size(ROW), aligned, weight_cols), padded.dtype)
    placed = lax.dynamic_update_slice_in_dim(placed, padded[None], lax.axis_index(ROW), 0)
    slabs = lax.psum(placed, ROW)
    largest = jnp.max(slabs[:, weight_rows].astype(jnp.float32), axis=0)

    def clipped_columns(first, last):
        part = slabs[:, :weight_rows, first:last].reshape(-1, last - first)
        return clip_with(part, largest[first:last])

    rows_tokens, piece = tokens.shape
    cores = lax.axis_size("cc")
    high = gain.astype(jnp.bfloat16)
    rest = gain - high.astype(jnp.float32)
    middle = rest.astype(jnp.bfloat16)
    low = (rest - middle.astype(jnp.float32)).astype(jnp.bfloat16)
    filler = jnp.zeros((GAIN_ROWS - 3, piece), jnp.bfloat16)
    packed = jnp.concatenate([tokens, high[None], middle[None], low[None], filler], axis=0)
    (along_y,) = ring_gather((packed,), "cy", (1,))
    (along_all,) = ring_gather((along_y,), "cc", (1,))
    blocks = along_all.shape[1] // (cores * piece)
    split = along_all[rows_tokens : rows_tokens + 3].astype(jnp.float32)
    full_gain = split[0] + (split[1] + split[2])
    widened = along_all[:rows_tokens].astype(jnp.float32)
    squares = jnp.sum(widened * widened, axis=1)
    inverse = lax.rsqrt(squares / D + EPS)[:, None]
    whole = (widened * inverse * full_gain[None, :]).astype(jnp.bfloat16)

    def ordered(first, last):
        part = clipped_columns(first, last)
        return (
            part.reshape(blocks, cores, piece, last - first)
            .transpose(1, 0, 2, 3)
            .reshape(part.shape)
        )

    kv_part = jnp.dot(whole, ordered(query_cols, weight_cols), preferred_element_type=jnp.float32)
    keys = kv_part[:, :key_cols]
    values = kv_part[:, key_cols:]
    query = jnp.dot(whole, ordered(0, query_cols), preferred_element_type=jnp.float32)
    heads_local = query_cols // HD
    kv_local = key_cols // HD
    group = heads_local // kv_local
    positions = lax.axis_index(ROW) * rows + jnp.arange(rows, dtype=jnp.int32)
    query = rotate(head_norm(query.reshape(rows, heads_local, HD), query_gain), positions).astype(
        jnp.bfloat16
    )
    keys = rotate(head_norm(keys.reshape(rows, kv_local, HD), key_gain), positions).astype(
        jnp.bfloat16
    )
    values = values.reshape(rows, kv_local, HD).astype(jnp.bfloat16)
    blocks_back = WINDOW // rows
    both = jnp.concatenate([keys, values], axis=1)
    earlier = [shifted(both, ROW, offset) for offset in range(blocks_back, 0, -1)]
    joined = jnp.concatenate(earlier + [both], axis=0)
    all_keys = joined[:, :kv_local]
    all_values = joined[:, kv_local:]
    key_pos = (
        positions[0] - blocks_back * rows + jnp.arange((blocks_back + 1) * rows, dtype=jnp.int32)
    )
    grouped = query.reshape(rows, kv_local, group, HD)
    scores = jnp.einsum(
        "tkgd,skd->kgts", grouped, all_keys, preferred_element_type=jnp.float32
    ) * QUERY_SCALAR ** (-0.5)
    distance = positions[:, None] - key_pos[None, :]
    allowed = (distance >= 0) & (distance < WINDOW) & (key_pos[None, :] >= 0)
    expo = jnp.where(allowed, jnp.exp(scores), 0.0)
    total = jnp.sum(expo, axis=-1, keepdims=True)
    probs = (expo / total).astype(jnp.bfloat16)
    output = jnp.einsum("kgts,skd->tkgd", probs, all_values, preferred_element_type=jnp.float32)
    return output.reshape(rows, query_cols).astype(jnp.bfloat16)


CORES_PER_CHIP = 2
GAIN_ROWS = 8
TILE_ROWS = 16


def solution(mesh):
    rows, cols = (mesh.shape["row"], mesh.shape["col"])
    minor = len({tuple(getattr(d, "coords", (0,)))[0] for d in mesh.devices[:, 0].flat})
    if rows % minor:
        minor = 1
    split = Mesh(
        mesh.devices.reshape(rows // minor, minor, cols // CORES_PER_CHIP, CORES_PER_CHIP),
        ("rz", "rx", "cy", "cc"),
    )
    col = ("cy", "cc")
    placed = (P(ROW, col), P(col), P(), P(), P(ROW, col), P(ROW, col), P(ROW, col))
    return jax.shard_map(local, mesh=split, in_specs=placed, out_specs=P(ROW, col), check_vma=False)
```

profile of v0, /device:TPU:1, one launch (start us, length us, event | category | flops | bytes accessed | tf_op | source)
XLA Modules:
  0.0 309.8 jit_solution(7325285267483653972)
XLA Ops:
  6.5 0.0 all-reduce.2.cloned.1.call-start
  6.5 0.8 subtract_convert_fusion.1
  7.3 1.2 copy.34
  8.5 0.3 concatenate.43
  8.8 4.0 %collective-permute-start.3 = (bf16[520,336]{1,0:T(8,128)(2,1)S(1)}, bf16[520,336]{1,0:T(8,128)(2,1)S(1)}, u32[]{:S(2)}, u32[]{:S(2)}) collective-permute-start(bf16[520,336]{1,0:T(8,128)(2,1)S(1)} %concatenate.43), channel_id=1, source_target_pairs={{0,2},{2,4},{4,6},{6,8},{8,10},{10,12},{12,14},{14,0},{1,3},{3,5},... | collective-permute-start | bytes 1048328 | tf_op jit(solution)/shard_map/ppermute | solution.py:30
  12.8 3.8 %collective-permute-start = (bf16[520,336]{1,0:T(8,128)(2,1)S(1)}, bf16[520,336]{1,0:T(8,128)(2,1)S(1)}, u32[]{:S(2)}, u32[]{:S(2)}) collective-permute-start(bf16[520,336]{1,0:T(8,128)(2,1)S(1)} %concatenate.43), channel_id=1, source_target_pairs={{0,14},{2,0},{4,2},{6,4},{8,6},{10,8},{12,10},{14,12},{1,15},{3,1}... | collective-permute-start | bytes 1048328 | tf_op jit(solution)/shard_map/ppermute | solution.py:33
  16.6 3.3 %collective-permute-done.3 = bf16[520,336]{1,0:T(8,128)(2,1)S(1)} collective-permute-done((bf16[520,336]{1,0:T(8,128)(2,1)S(1)}, bf16[520,336]{1,0:T(8,128)(2,1)S(1)}, u32[]{:S(2)}, u32[]{:S(2)}) %collective-permute-start.3) | collective-permute-done | bytes 349472 | tf_op jit(solution)/shard_map/ppermute | solution.py:30
  19.9 4.0 %collective-permute-start.4 = (bf16[520,336]{1,0:T(8,128)(2,1)S(1)}, bf16[520,336]{1,0:T(8,128)(2,1)S(1)}, u32[]{:S(2)}, u32[]{:S(2)}) collective-permute-start(bf16[520,336]{1,0:T(8,128)(2,1)S(1)} %collective-permute-done.3), channel_id=1, source_target_pairs={{0,2},{2,4},{4,6},{6,8},{8,10},{10,12},{12,14},{14,0},{1,3},{3,5},... | collective-permute-start | bytes 1048328 | tf_op jit(solution)/shard_map/ppermute | solution.py:30
  23.9 0.0 collective-permute-done
  23.9 4.7 %collective-permute-start.1 = (bf16[520,336]{1,0:T(8,128)(2,1)S(1)}, bf16[520,336]{1,0:T(8,128)(2,1)S(1)}, u32[]{:S(2)}, u32[]{:S(2)}) collective-permute-start(bf16[520,336]{1,0:T(8,128)(2,1)S(1)} %collective-permute-done), channel_id=1, source_target_pairs={{0,14},{2,0},{4,2},{6,4},{8,6},{10,8},{12,10},{14,12},{1,15},{3,1}... | collective-permute-start | bytes 1048328 | tf_op jit(solution)/shard_map/ppermute | solution.py:33
  28.7 3.3 %collective-permute-done.4 = bf16[520,336]{1,0:T(8,128)(2,1)S(1)} collective-permute-done((bf16[520,336]{1,0:T(8,128)(2,1)S(1)}, bf16[520,336]{1,0:T(8,128)(2,1)S(1)}, u32[]{:S(2)}, u32[]{:S(2)}) %collective-permute-start.4) | collective-permute-done | bytes 349472 | tf_op jit(solution)/shard_map/ppermute | solution.py:30
  31.9 3.1 collective-permute-start.5
  35.0 0.9 constant_dynamic-update-slice_fusion.2
  35.9 0.0 collective-permute-done.1
  35.9 4.7 %collective-permute-start.2 = (bf16[520,336]{1,0:T(8,128)(2,1)S(1)}, bf16[520,336]{1,0:T(8,128)(2,1)S(1)}, u32[]{:S(2)}, u32[]{:S(2)}) collective-permute-start(bf16[520,336]{1,0:T(8,128)(2,1)S(1)} %collective-permute-done.1), channel_id=1, source_target_pairs={{0,14},{2,0},{4,2},{6,4},{8,6},{10,8},{12,10},{14,12},{1,15},{3,1}... | collective-permute-start | bytes 1048328 | tf_op jit(solution)/shard_map/ppermute | solution.py:33
  40.6 2.4 collective-permute-done.5
  43.0 2.1 collective-permute-start.6
  45.2 0.8 constant_dynamic-update-slice_fusion.1
  46.0 0.8 constant_dynamic-update-slice_fusion
  46.8 0.1 pad.12.clone
  46.9 0.0 collective-permute-done.2
  46.9 6.3 %collective-permute-done.6 = bf16[520,336]{1,0:T(8,128)(2,1)S(1)} collective-permute-done((bf16[520,336]{1,0:T(8,128)(2,1)S(1)}, bf16[520,336]{1,0:T(8,128)(2,1)S(1)}, u32[]{:S(2)}, u32[]{:S(2)}) %collective-permute-start.6) | collective-permute-done | bytes 349472 | tf_op jit(solution)/shard_map/ppermute | solution.py:30
  53.2 7.6 %concatenate.44 = bf16[520,5376]{1,0:T(8,128)(2,1)} concatenate(bf16[520,336]{1,0:T(8,128)(2,1)S(1)} %concatenate.43, bf16[520,336]{1,0:T(8,128)(2,1)S(1)} %collective-permute-done, bf16[520,336]{1,0:T(8,128)(2,1)S(1)} %collective-permute-done.1, bf16[520,336]{1,0:T(8,128)(2,1)S(1)} %collective-permute-done.2, bf16[520,336]{1,0:T(8,128)(2,1)S(1)} %collective-permute-done.6, ...), dimensions={1} | concatenate | bytes 11182080 | tf_op jit(solution)/shard_map/concatenate | solution.py:39
  60.7 3.3 %constant_dynamic-slice_fusion = bf16[520,2688]{1,0:T(8,128)(2,1)S(1)} fusion(bf16[520,5376]{1,0:T(8,128)(2,1)} %concatenate.44, s32[]{:T(128)S(6)} %select_n.25), kind=kLoop, calls=%fused_computation.80 | loop fusion | bytes 5591044 | tf_op jit(solution)/shard_map/dynamic_slice | solution.py:41
  64.0 8.3 %collective-permute-start.7 = (bf16[520,2688]{1,0:T(8,128)(2,1)S(1)}, bf16[520,2688]{1,0:T(8,128)(2,1)}, u32[]{:S(2)}, u32[]{:S(2)}) collective-permute-start(bf16[520,2688]{1,0:T(8,128)(2,1)S(1)} %constant_dynamic-slice_fusion), channel_id=1, source_target_pairs={{0,1},{1,0},{2,3},{3,2},{4,5},{5,4},{6,7},{7,6},{8,9},{9,8},{10,11... | collective-permute-start | bytes 8386568 | tf_op jit(solution)/shard_map/ppermute | solution.py:30
  72.4 3.2 %broadcast_in_dim.60 = bf16[32,176,512]{2,1,0:T(8,128)(2,1)} broadcast(bf16[]{:T(256)} %constant.29.clone.1), dimensions={} | broadcast | bytes 5767170 | tf_op jit(solution)/shard_map/broadcast_in_dim | solution.py:87
  75.6 0.8 fusion.33
  76.4 0.0 all-reduce.2.cloned.1.call-update
  76.4 0.5 slice.71
  77.6 0.5 multiply_cosine_fusion
  78.2 2.0 fusion.16
  80.2 0.0 collective-permute-done.7
  80.2 5.2 %fusion.5 = bf16[520,5376]{1,0:T(8,128)(2,1)S(1)} fusion(s32[]{:T(128)S(6)} %select_n.27, bf16[520,2688]{1,0:T(8,128)(2,1)S(1)} %constant_dynamic-slice_fusion, bf16[520,2688]{1,0:T(8,128)(2,1)} %collective-permute-done.7), kind=kLoop, calls=%fused_computation.13 | loop fusion | flops 22364160 | bytes 11182084 | tf_op jit(solution)/shard_map/concatenate | solution.py:39
  85.3 0.0 copy-start
  85.4 0.1 fusion.40
  85.4 2.3 copy-done
  87.7 1.2 fusion
  88.9 182.9 %all-reduce.2.cloned.1.call-done = bf16[32,176,512]{2,1,0:T(8,128)(2,1)} async-done(((bf16[32,176,512]{2,1,0:T(8,128)(2,1)}), bf16[32,176,512]{2,1,0:T(8,128)(2,1)}) %all-reduce.2.cloned.1.call-update) | async-done | bytes 5767184 | tf_op jit(solution)/shard_map/psum | solution.py:89
  271.8 1.0 slice_reduce_fusion
  272.9 0.0 slice-start
  272.9 3.2 %fusion.48 = (bf16[32,168,256]{2,1,0:T(8,128)(2,1)S(1)}, bf16[32,168,256]{2,1,0:T(8,128)(2,1)S(1)}) fusion(bf16[32,176,512]{2,1,0:T(8,128)(2,1)} %all-reduce.2.cloned.1.call-done), kind=kLoop, calls=%fused_computation.91 | loop fusion | bytes 11010048 | tf_op jit(solution)/shard_map/slice | solution.py:93
  276.0 0.0 slice-start.1
  276.0 1.3 fusion.17
  277.3 0.2 copy.35
  277.5 0.0 copy-done.2
  277.5 0.0 slice-done
  277.5 0.0 slice-done.1
  277.6 2.0 fusion.23
  279.7 0.1 multiply_bitcast_fusion
  279.8 0.6 fusion.35
  280.4 5.4 %collective-permute-start.8 = (bf16[512,2,128]{0,2,1:T(8,128)(2,1)S(1)}, bf16[512,2,128]{0,2,1:T(8,128)(2,1)}, u32[]{:S(2)}, u32[]{:S(2)}) collective-permute-start(bf16[512,2,128]{0,2,1:T(8,128)(2,1)S(1)} %pad_maximum_fusion), channel_id=1, source_target_pairs={{0,32},{16,48},{32,64},{48,80},{64,96},{80,112},{96,128},{112,144}... | collective-permute-start | bytes 786440 | tf_op jit(solution)/shard_map/ppermute | solution.py:19
  285.7 2.9 collective-permute-start.9
  288.6 0.2 copy.36
  288.8 3.0 copy.46
  291.8 5.2 %multiply_reduce_fusion = (f32[512,2]{0,1:T(2,128)S(1)}, f32[512,2,128]{0,2,1:T(8,128)S(1)}) fusion(bf16[2,128,5376]{2,1,0:T(8,128)(2,1)} %bitcast.68, f32[5376]{0:T(1024)} %copy-done.2, f32[512]{0:T(512)S(1)} %add_rsqrt_fusion.2, bf16[520,5376]{1,0:T(8,128)(2,1)} %copy-done), kind=kOutput, calls=%fused_computation.35 | convolution fusion | flops 1420557312 | bytes 8812544 | tf_op jit(solution)/shard_map/dot_general | solution.py:125
  297.0 0.1 multiply_multiply_fusion
  297.1 0.1 subtract_convert_fusion
  297.2 0.0 collective-permute-done.8
  297.2 0.0 collective-permute-done.9
  297.3 1.1 maximum_maximum_fusion
  298.3 0.0 copy-done.1
  298.4 1.7 fusion.12
  300.1 2.0 fusion.19
  302.1 0.8 copy.41
  (28 shorter events, 0.2 us)
Async XLA Ops:
  6.5 265.3 %all-reduce.2.cloned.1.call-start = ((), (), s32[]{:S(2)}) async-start(), calls=%async_computation | async-start | bytes 11534336 | tf_op jit(solution)/shard_map/psum | solution.py:89
  8.8 11.1 %collective-permute-start.3 = (bf16[520,336]{1,0:T(8,128)(2,1)S(1)}, bf16[520,336]{1,0:T(8,128)(2,1)S(1)}, u32[]{:S(2)}, u32[]{:S(2)}) collective-permute-start(bf16[520,336]{1,0:T(8,128)(2,1)S(1)} %concatenate.43), channel_id=1, source_target_pairs={{0,2},{2,4},{4,6},{6,8},{8,10},{10,12},{12,14},{14,0},{1,3},{3,5},... | collective-permute-start | bytes 1048328 | tf_op jit(solution)/shard_map/ppermute | solution.py:30
  12.8 11.1 %collective-permute-start = (bf16[520,336]{1,0:T(8,128)(2,1)S(1)}, bf16[520,336]{1,0:T(8,128)(2,1)S(1)}, u32[]{:S(2)}, u32[]{:S(2)}) collective-permute-start(bf16[520,336]{1,0:T(8,128)(2,1)S(1)} %concatenate.43), channel_id=1, source_target_pairs={{0,14},{2,0},{4,2},{6,4},{8,6},{10,8},{12,10},{14,12},{1,15},{3,1}... | collective-permute-start | bytes 1048328 | tf_op jit(solution)/shard_map/ppermute | solution.py:33
  19.9 12.0 %collective-permute-start.4 = (bf16[520,336]{1,0:T(8,128)(2,1)S(1)}, bf16[520,336]{1,0:T(8,128)(2,1)S(1)}, u32[]{:S(2)}, u32[]{:S(2)}) collective-permute-start(bf16[520,336]{1,0:T(8,128)(2,1)S(1)} %collective-permute-done.3), channel_id=1, source_target_pairs={{0,2},{2,4},{4,6},{6,8},{8,10},{10,12},{12,14},{14,0},{1,3},{3,5},... | collective-permute-start | bytes 1048328 | tf_op jit(solution)/shard_map/ppermute | solution.py:30
  23.9 12.0 %collective-permute-start.1 = (bf16[520,336]{1,0:T(8,128)(2,1)S(1)}, bf16[520,336]{1,0:T(8,128)(2,1)S(1)}, u32[]{:S(2)}, u32[]{:S(2)}) collective-permute-start(bf16[520,336]{1,0:T(8,128)(2,1)S(1)} %collective-permute-done), channel_id=1, source_target_pairs={{0,14},{2,0},{4,2},{6,4},{8,6},{10,8},{12,10},{14,12},{1,15},{3,1}... | collective-permute-start | bytes 1048328 | tf_op jit(solution)/shard_map/ppermute | solution.py:33
  31.9 11.1 %collective-permute-start.5 = (bf16[520,336]{1,0:T(8,128)(2,1)S(1)}, bf16[520,336]{1,0:T(8,128)(2,1)S(1)}, u32[]{:S(2)}, u32[]{:S(2)}) collective-permute-start(bf16[520,336]{1,0:T(8,128)(2,1)S(1)} %collective-permute-done.4), channel_id=1, source_target_pairs={{0,2},{2,4},{4,6},{6,8},{8,10},{10,12},{12,14},{14,0},{1,3},{3,5},... | collective-permute-start | bytes 1048328 | tf_op jit(solution)/shard_map/ppermute | solution.py:30
  35.9 11.0 %collective-permute-start.2 = (bf16[520,336]{1,0:T(8,128)(2,1)S(1)}, bf16[520,336]{1,0:T(8,128)(2,1)S(1)}, u32[]{:S(2)}, u32[]{:S(2)}) collective-permute-start(bf16[520,336]{1,0:T(8,128)(2,1)S(1)} %collective-permute-done.1), channel_id=1, source_target_pairs={{0,14},{2,0},{4,2},{6,4},{8,6},{10,8},{12,10},{14,12},{1,15},{3,1}... | collective-permute-start | bytes 1048328 | tf_op jit(solution)/shard_map/ppermute | solution.py:33
  43.0 10.2 %collective-permute-start.6 = (bf16[520,336]{1,0:T(8,128)(2,1)S(1)}, bf16[520,336]{1,0:T(8,128)(2,1)S(1)}, u32[]{:S(2)}, u32[]{:S(2)}) collective-permute-start(bf16[520,336]{1,0:T(8,128)(2,1)S(1)} %collective-permute-done.5), channel_id=1, source_target_pairs={{0,2},{2,4},{4,6},{6,8},{8,10},{10,12},{12,14},{14,0},{1,3},{3,5},... | collective-permute-start | bytes 1048328 | tf_op jit(solution)/shard_map/ppermute | solution.py:30
  64.0 16.1 %collective-permute-start.7 = (bf16[520,2688]{1,0:T(8,128)(2,1)S(1)}, bf16[520,2688]{1,0:T(8,128)(2,1)}, u32[]{:S(2)}, u32[]{:S(2)}) collective-permute-start(bf16[520,2688]{1,0:T(8,128)(2,1)S(1)} %constant_dynamic-slice_fusion), channel_id=1, source_target_pairs={{0,1},{1,0},{2,3},{3,2},{4,5},{5,4},{6,7},{7,6},{8,9},{9,8},{10,11... | collective-permute-start | bytes 8386568 | tf_op jit(solution)/shard_map/ppermute | solution.py:30
  85.3 2.4 copy-start
  87.7 189.8 %copy-start.2 = (f32[5376]{0:T(1024)}, f32[5376]{0:T(1024)S(1)}, u32[]{:S(2)}) copy-start(f32[5376]{0:T(1024)S(1)} %fusion.40) | copy-start | bytes 64516
  272.9 4.6 %slice-start = ((s8[5591040]{0:T(1024)(128)(4,1)}), s8[4194304]{0:T(1024)(128)(4,1)S(1)}, s32[]{:S(2)}) async-start(s8[5591040]{0:T(1024)(128)(4,1)} %bitcast.63), calls=%async_computation.1 | async-start | bytes 8388608
  276.0 1.5 slice-start.1
  277.5 2.1 copy-start.3
  280.4 16.9 %collective-permute-start.8 = (bf16[512,2,128]{0,2,1:T(8,128)(2,1)S(1)}, bf16[512,2,128]{0,2,1:T(8,128)(2,1)}, u32[]{:S(2)}, u32[]{:S(2)}) collective-permute-start(bf16[512,2,128]{0,2,1:T(8,128)(2,1)S(1)} %pad_maximum_fusion), channel_id=1, source_target_pairs={{0,32},{16,48},{32,64},{48,80},{64,96},{80,112},{96,128},{112,144}... | collective-permute-start | bytes 786440 | tf_op jit(solution)/shard_map/ppermute | solution.py:19
  285.7 11.5 %collective-permute-start.9 = (bf16[512,2,128]{0,2,1:T(8,128)(2,1)S(1)}, bf16[512,2,128]{0,2,1:T(8,128)(2,1)}, u32[]{:S(2)}, u32[]{:S(2)}) collective-permute-start(bf16[512,2,128]{0,2,1:T(8,128)(2,1)S(1)} %pad_maximum_fusion), channel_id=1, source_target_pairs={{0,16},{16,32},{32,48},{48,64},{64,80},{80,96},{96,112},{112,128},... | collective-permute-start | bytes 786440 | tf_op jit(solution)/shard_map/ppermute | solution.py:19
  291.8 5.2 %copy-start.4 = (f32[128]{0:T(128)S(1)}, f32[128]{0:T(128)}, u32[]{:S(2)}) copy-start(f32[128]{0:T(128)} %param.9) | copy-start | bytes 1540
  291.8 6.5 %copy-start.1 = (pred[512,1536]{0,1:T(8,128)(4,1)S(1)}, pred[512,1536]{0,1:T(8,128)(4,1)}, u32[]{:S(2)}) copy-start(pred[512,1536]{0,1:T(8,128)(4,1)} %fusion.16) | copy-start | bytes 2359300
Sparse Core Ops, SparseCore 0:
  76.5 195.2 all-reduce.1
where the time goes:
time: 310 us
  waiting for transfers between devices  198 us (64%)
  starting transfers between devices  43.1 us (14%)
  local copies, waits for them, and re-layouts  28.3 us (9%)
  other arithmetic  14.8 us (5%)
  between operations  14.5 us (5%)
  matrix products  10.9 us (4%)
    psum x1, waiting for transfers between devices, local(): slabs = lax.psum(placed, ROW)  183 us
    ppermute x5, starting transfers between devices, ring_gather(): forward = lax.ppermute(forward, axis, right)  21.5 us
    ppermute x5, waiting for transfers between devices, ring_gather(): forward = lax.ppermute(forward, axis, right)  15.2 us
    ppermute x3, starting transfers between devices, ring_gather(): backward = lax.ppermute(backward, axis, left)  13.2 us
    ppermute x2, starting transfers between devices, shifted(): return lax.ppermute(array, axis, pairs)  8.27 us
    concatenate x1, local copies, waits for them, and re-layouts, ring_gather(): doubled = jnp.concatenate([stacked, stacked], axis=dim)  7.58 us
  transfers between devices with their start and end apart: 11, of which 5 were waited for; matrix products, arithmetic and copies ran while one was open for 8% of the time, Pallas kernels for 0%

commit v1 on v0

--- a/solution.py
+++ b/solution.py
@@ -86,7 +86,7 @@
     )
     placed = jnp.zeros((lax.axis_size(ROW), aligned, weight_cols), padded.dtype)
     placed = lax.dynamic_update_slice_in_dim(placed, padded[None], lax.axis_index(ROW), 0)
-    slabs = lax.psum(placed, ROW)
+    slabs = lax.psum(lax.psum(placed, "rz"), "rx")
     largest = jnp.max(slabs[:, weight_rows].astype(jnp.float32), axis=0)
 
     def clipped_columns(first, last):

time: 310 us -> 332 us (1.071)
  waiting for transfers between devices: 198 us -> 222 us
    psum x1 -> x2, waiting for transfers between devices: 183 us -> 203 us  [local(): slabs = lax.psum(lax.psum(placed, 'rz'), 'rx')]
  transfers between devices with their start and end apart: 11 -> 12, of which waited for: 5 -> 7; matrix products, arithmetic and copies ran while one was open for 8% -> 9% of each run, Pallas kernels for 0% -> 0%
where the time goes in v1:
time: 332 us; the launch traced here: 330 us
  waiting for transfers between devices  222 us (67%)
  starting transfers between devices  40.4 us (12%)
  local copies, waits for them, and re-layouts  27.4 us (8%)
  between operations  14.5 us (4%)
  other arithmetic  14.1 us (4%)
  matrix products  10.9 us (3%)
    psum x2, waiting for transfers between devices, local(): slabs = lax.psum(lax.psum(placed, 'rz'), 'rx')  203 us
    ppermute x5, starting transfers between devices, ring_gather(): forward = lax.ppermute(forward, axis, right)  20.6 us
    ppermute x5, waiting for transfers between devices, ring_gather(): forward = lax.ppermute(forward, axis, right)  16.8 us
    ppermute x3, starting transfers between devices, ring_gather(): backward = lax.ppermute(backward, axis, left)  13.4 us
    concatenate x1, local copies, waits for them, and re-layouts, ring_gather(): doubled = jnp.concatenate([stacked, stacked], axis=dim)  7.61 us
  transfers between devices with their start and end apart: 12, of which 7 were waited for; matrix products, arithmetic and copies ran while one was open for 9% of the time, Pallas kernels for 0%

profile of v1, /device:TPU:1, one launch (start us, length us, event | category | flops | bytes accessed | tf_op | source)
XLA Modules:
  0.0 329.5 jit_solution(17440105268959421789)
XLA Ops:
  6.5 0.0 all-reduce.3.cloned.1.call-start
  6.5 0.9 constant_dynamic-update-slice_fusion.2
  7.4 0.8 constant_dynamic-update-slice_fusion.1
  8.2 0.8 constant_dynamic-update-slice_fusion
  9.1 0.1 pad.12.clone
  9.2 3.2 broadcast_in_dim.60
  12.4 0.8 fusion.33
  13.1 0.0 all-reduce.3.cloned.1.call-update
  13.2 0.0 all-reduce.5.cloned.1.call-start
  13.3 0.0 copy-done.2
  13.3 0.2 copy.34
  13.5 0.3 concatenate.43
  13.8 4.0 %collective-permute-start.3 = (bf16[520,336]{1,0:T(8,128)(2,1)S(1)}, bf16[520,336]{1,0:T(8,128)(2,1)S(1)}, u32[]{:S(2)}, u32[]{:S(2)}) collective-permute-start(bf16[520,336]{1,0:T(8,128)(2,1)S(1)} %concatenate.43), channel_id=1, source_target_pairs={{0,2},{2,4},{4,6},{6,8},{8,10},{10,12},{12,14},{14,0},{1,3},{3,5},... | collective-permute-start | bytes 1048328 | tf_op jit(solution)/shard_map/ppermute | solution.py:30
  17.8 3.8 %collective-permute-start = (bf16[520,336]{1,0:T(8,128)(2,1)S(1)}, bf16[520,336]{1,0:T(8,128)(2,1)S(1)}, u32[]{:S(2)}, u32[]{:S(2)}) collective-permute-start(bf16[520,336]{1,0:T(8,128)(2,1)S(1)} %concatenate.43), channel_id=1, source_target_pairs={{0,14},{2,0},{4,2},{6,4},{8,6},{10,8},{12,10},{14,12},{1,15},{3,1}... | collective-permute-start | bytes 1048328 | tf_op jit(solution)/shard_map/ppermute | solution.py:33
  21.6 3.3 collective-permute-done.3
  24.9 4.0 %collective-permute-start.4 = (bf16[520,336]{1,0:T(8,128)(2,1)S(1)}, bf16[520,336]{1,0:T(8,128)(2,1)S(1)}, u32[]{:S(2)}, u32[]{:S(2)}) collective-permute-start(bf16[520,336]{1,0:T(8,128)(2,1)S(1)} %collective-permute-done.3), channel_id=1, source_target_pairs={{0,2},{2,4},{4,6},{6,8},{8,10},{10,12},{12,14},{14,0},{1,3},{3,5},... | collective-permute-start | bytes 1048328 | tf_op jit(solution)/shard_map/ppermute | solution.py:30
  28.9 0.0 collective-permute-done
  28.9 4.7 %collective-permute-start.1 = (bf16[520,336]{1,0:T(8,128)(2,1)S(1)}, bf16[520,336]{1,0:T(8,128)(2,1)S(1)}, u32[]{:S(2)}, u32[]{:S(2)}) collective-permute-start(bf16[520,336]{1,0:T(8,128)(2,1)S(1)} %collective-permute-done), channel_id=1, source_target_pairs={{0,14},{2,0},{4,2},{6,4},{8,6},{10,8},{12,10},{14,12},{1,15},{3,1}... | collective-permute-start | bytes 1048328 | tf_op jit(solution)/shard_map/ppermute | solution.py:33
  33.6 3.3 collective-permute-done.4
  36.9 3.1 collective-permute-start.5
  40.0 0.0 collective-permute-done.1
  40.0 4.8 %collective-permute-start.2 = (bf16[520,336]{1,0:T(8,128)(2,1)S(1)}, bf16[520,336]{1,0:T(8,128)(2,1)S(1)}, u32[]{:S(2)}, u32[]{:S(2)}) collective-permute-start(bf16[520,336]{1,0:T(8,128)(2,1)S(1)} %collective-permute-done.1), channel_id=1, source_target_pairs={{0,14},{2,0},{4,2},{6,4},{8,6},{10,8},{12,10},{14,12},{1,15},{3,1}... | collective-permute-start | bytes 1048328 | tf_op jit(solution)/shard_map/ppermute | solution.py:33
  44.8 3.7 %collective-permute-done.5 = bf16[520,336]{1,0:T(8,128)(2,1)S(1)} collective-permute-done((bf16[520,336]{1,0:T(8,128)(2,1)S(1)}, bf16[520,336]{1,0:T(8,128)(2,1)S(1)}, u32[]{:S(2)}, u32[]{:S(2)}) %collective-permute-start.5) | collective-permute-done | bytes 349472 | tf_op jit(solution)/shard_map/ppermute | solution.py:30
  48.5 1.9 collective-permute-start.6
  50.4 1.9 collective-permute-done.2
  52.3 6.6 %collective-permute-done.6 = bf16[520,336]{1,0:T(8,128)(2,1)S(1)} collective-permute-done((bf16[520,336]{1,0:T(8,128)(2,1)S(1)}, bf16[520,336]{1,0:T(8,128)(2,1)S(1)}, u32[]{:S(2)}, u32[]{:S(2)}) %collective-permute-start.6) | collective-permute-done | bytes 349472 | tf_op jit(solution)/shard_map/ppermute | solution.py:30
  58.9 7.6 %concatenate.44 = bf16[520,5376]{1,0:T(8,128)(2,1)} concatenate(bf16[520,336]{1,0:T(8,128)(2,1)S(1)} %concatenate.43, bf16[520,336]{1,0:T(8,128)(2,1)S(1)} %collective-permute-done, bf16[520,336]{1,0:T(8,128)(2,1)S(1)} %collective-permute-done.1, bf16[520,336]{1,0:T(8,128)(2,1)S(1)} %collective-permute-done.2, bf16[520,336]{1,0:T(8,128)(2,1)S(1)} %collective-permute-done.6, ...), dimensions={1} | concatenate | bytes 11182080 | tf_op jit(solution)/shard_map/concatenate | solution.py:39
  66.5 3.3 %constant_dynamic-slice_fusion = bf16[520,2688]{1,0:T(8,128)(2,1)S(1)} fusion(bf16[520,5376]{1,0:T(8,128)(2,1)} %concatenate.44, s32[]{:T(128)S(6)} %select_n.25), kind=kLoop, calls=%fused_computation.80 | loop fusion | bytes 5591044 | tf_op jit(solution)/shard_map/dynamic_slice | solution.py:41
  69.8 7.6 %collective-permute-start.7 = (bf16[520,2688]{1,0:T(8,128)(2,1)S(1)}, bf16[520,2688]{1,0:T(8,128)(2,1)}, u32[]{:S(2)}, u32[]{:S(2)}) collective-permute-start(bf16[520,2688]{1,0:T(8,128)(2,1)S(1)} %constant_dynamic-slice_fusion), channel_id=1, source_target_pairs={{0,1},{1,0},{2,3},{3,2},{4,5},{5,4},{6,7},{7,6},{8,9},{9,8},{10,11... | collective-permute-start | bytes 8386568 | tf_op jit(solution)/shard_map/ppermute | solution.py:30
  77.4 86.4 %all-reduce.3.cloned.1.call-done = bf16[32,176,512]{2,1,0:T(8,128)(2,1)} async-done(((bf16[32,176,512]{2,1,0:T(8,128)(2,1)}), bf16[32,176,512]{2,1,0:T(8,128)(2,1)}) %all-reduce.3.cloned.1.call-update) | async-done | bytes 5767184 | tf_op jit(solution)/shard_map/psum | solution.py:89
  163.8 0.0 all-reduce.5.cloned.1.call-update
  163.8 0.5 slice.71
  165.1 0.5 multiply_cosine_fusion
  165.6 2.0 fusion.16
  167.6 0.0 collective-permute-done.7
  167.6 5.2 %fusion.5 = bf16[520,5376]{1,0:T(8,128)(2,1)S(1)} fusion(s32[]{:T(128)S(6)} %select_n.27, bf16[520,2688]{1,0:T(8,128)(2,1)S(1)} %constant_dynamic-slice_fusion, bf16[520,2688]{1,0:T(8,128)(2,1)} %collective-permute-done.7), kind=kLoop, calls=%fused_computation.13 | loop fusion | flops 22364160 | bytes 11182084 | tf_op jit(solution)/shard_map/concatenate | solution.py:39
  172.7 0.0 copy-start
  172.8 0.1 fusion.40
  172.9 2.3 copy-done
  175.1 1.2 fusion
  176.3 117.1 %all-reduce.5.cloned.1.call-done = bf16[32,176,512]{2,1,0:T(8,128)(2,1)} async-done(((bf16[32,176,512]{2,1,0:T(8,128)(2,1)}), bf16[32,176,512]{2,1,0:T(8,128)(2,1)}) %all-reduce.5.cloned.1.call-update) | async-done | bytes 5767184 | tf_op jit(solution)/shard_map/psum | solution.py:89
  293.4 1.0 slice_reduce_fusion
  294.5 0.0 slice-start
  294.5 3.2 fusion.48
  297.6 0.0 slice-start.1
  297.6 1.3 fusion.17
  298.9 0.2 copy.35
  299.1 0.0 slice-done.1
  299.2 2.0 fusion.23
  301.3 0.1 multiply_bitcast_fusion
  301.4 0.6 fusion.35
  302.0 4.0 %collective-permute-start.8 = (bf16[512,2,128]{0,2,1:T(8,128)(2,1)S(1)}, bf16[512,2,128]{0,2,1:T(8,128)(2,1)}, u32[]{:S(2)}, u32[]{:S(2)}) collective-permute-start(bf16[512,2,128]{0,2,1:T(8,128)(2,1)S(1)} %pad_maximum_fusion), channel_id=1, source_target_pairs={{0,32},{16,48},{32,64},{48,80},{64,96},{80,112},{96,128},{112,144}... | collective-permute-start | bytes 786440 | tf_op jit(solution)/shard_map/ppermute | solution.py:19
  306.0 2.4 collective-permute-start.9
  308.4 0.2 copy.36
  308.6 3.0 copy.46
  311.6 5.2 %multiply_reduce_fusion = (f32[512,2]{0,1:T(2,128)S(1)}, f32[512,2,128]{0,2,1:T(8,128)S(1)}) fusion(bf16[2,128,5376]{2,1,0:T(8,128)(2,1)} %bitcast.68, f32[5376]{0:T(1024)} %copy-done.3, f32[512]{0:T(512)S(1)} %add_rsqrt_fusion.2, bf16[520,5376]{1,0:T(8,128)(2,1)} %copy-done), kind=kOutput, calls=%fused_computation.35 | convolution fusion | flops 1420557312 | bytes 8812544 | tf_op jit(solution)/shard_map/dot_general | solution.py:125
  316.8 0.1 multiply_multiply_fusion
  316.9 0.1 subtract_convert_fusion
  317.0 0.0 collective-permute-done.8
  317.0 0.0 collective-permute-done.9
  317.0 1.1 maximum_maximum_fusion
  318.1 1.7 fusion.12
  319.8 2.0 fusion.19
  321.8 0.8 copy.41
  (35 shorter events, 0.3 us)
Async XLA Ops:
  6.5 157.3 %all-reduce.3.cloned.1.call-start = ((), (), s32[]{:S(2)}) async-start(), calls=%async_computation | async-start | bytes 11534336 | tf_op jit(solution)/shard_map/psum | solution.py:89
  9.2 4.0 %copy-start.4 = (f32[336]{0:T(512)S(1)}, f32[336]{0:T(512)}, u32[]{:S(2)}) copy-start(f32[336]{0:T(512)} %param.8) | copy-start | bytes 4036
  9.2 4.1 %copy-start.2 = (bf16[512,336]{0,1:T(8,128)(2,1)S(1)}, bf16[512,336]{0,1:T(8,128)(2,1)}, u32[]{:S(2)}) copy-start(bf16[512,336]{0,1:T(8,128)(2,1)} %param.7) | copy-start | bytes 1032196
  13.2 280.2 %all-reduce.5.cloned.1.call-start = ((), (), s32[]{:S(2)}) async-start(), calls=%async_computation.1 | async-start | bytes 11534336 | tf_op jit(solution)/shard_map/psum | solution.py:89
  13.8 11.1 %collective-permute-start.3 = (bf16[520,336]{1,0:T(8,128)(2,1)S(1)}, bf16[520,336]{1,0:T(8,128)(2,1)S(1)}, u32[]{:S(2)}, u32[]{:S(2)}) collective-permute-start(bf16[520,336]{1,0:T(8,128)(2,1)S(1)} %concatenate.43), channel_id=1, source_target_pairs={{0,2},{2,4},{4,6},{6,8},{8,10},{10,12},{12,14},{14,0},{1,3},{3,5},... | collective-permute-start | bytes 1048328 | tf_op jit(solution)/shard_map/ppermute | solution.py:30
  17.8 11.1 %collective-permute-start = (bf16[520,336]{1,0:T(8,128)(2,1)S(1)}, bf16[520,336]{1,0:T(8,128)(2,1)S(1)}, u32[]{:S(2)}, u32[]{:S(2)}) collective-permute-start(bf16[520,336]{1,0:T(8,128)(2,1)S(1)} %concatenate.43), channel_id=1, source_target_pairs={{0,14},{2,0},{4,2},{6,4},{8,6},{10,8},{12,10},{14,12},{1,15},{3,1}... | collective-permute-start | bytes 1048328 | tf_op jit(solution)/shard_map/ppermute | solution.py:33
  24.9 12.0 %collective-permute-start.4 = (bf16[520,336]{1,0:T(8,128)(2,1)S(1)}, bf16[520,336]{1,0:T(8,128)(2,1)S(1)}, u32[]{:S(2)}, u32[]{:S(2)}) collective-permute-start(bf16[520,336]{1,0:T(8,128)(2,1)S(1)} %collective-permute-done.3), channel_id=1, source_target_pairs={{0,2},{2,4},{4,6},{6,8},{8,10},{10,12},{12,14},{14,0},{1,3},{3,5},... | collective-permute-start | bytes 1048328 | tf_op jit(solution)/shard_map/ppermute | solution.py:30
  28.9 11.1 %collective-permute-start.1 = (bf16[520,336]{1,0:T(8,128)(2,1)S(1)}, bf16[520,336]{1,0:T(8,128)(2,1)S(1)}, u32[]{:S(2)}, u32[]{:S(2)}) collective-permute-start(bf16[520,336]{1,0:T(8,128)(2,1)S(1)} %collective-permute-done), channel_id=1, source_target_pairs={{0,14},{2,0},{4,2},{6,4},{8,6},{10,8},{12,10},{14,12},{1,15},{3,1}... | collective-permute-start | bytes 1048328 | tf_op jit(solution)/shard_map/ppermute | solution.py:33
  36.9 11.6 %collective-permute-start.5 = (bf16[520,336]{1,0:T(8,128)(2,1)S(1)}, bf16[520,336]{1,0:T(8,128)(2,1)S(1)}, u32[]{:S(2)}, u32[]{:S(2)}) collective-permute-start(bf16[520,336]{1,0:T(8,128)(2,1)S(1)} %collective-permute-done.4), channel_id=1, source_target_pairs={{0,2},{2,4},{4,6},{6,8},{8,10},{10,12},{12,14},{14,0},{1,3},{3,5},... | collective-permute-start | bytes 1048328 | tf_op jit(solution)/shard_map/ppermute | solution.py:30
  40.0 12.3 %collective-permute-start.2 = (bf16[520,336]{1,0:T(8,128)(2,1)S(1)}, bf16[520,336]{1,0:T(8,128)(2,1)S(1)}, u32[]{:S(2)}, u32[]{:S(2)}) collective-permute-start(bf16[520,336]{1,0:T(8,128)(2,1)S(1)} %collective-permute-done.1), channel_id=1, source_target_pairs={{0,14},{2,0},{4,2},{6,4},{8,6},{10,8},{12,10},{14,12},{1,15},{3,1}... | collective-permute-start | bytes 1048328 | tf_op jit(solution)/shard_map/ppermute | solution.py:33
  48.5 10.4 %collective-permute-start.6 = (bf16[520,336]{1,0:T(8,128)(2,1)S(1)}, bf16[520,336]{1,0:T(8,128)(2,1)S(1)}, u32[]{:S(2)}, u32[]{:S(2)}) collective-permute-start(bf16[520,336]{1,0:T(8,128)(2,1)S(1)} %collective-permute-done.5), channel_id=1, source_target_pairs={{0,2},{2,4},{4,6},{6,8},{8,10},{10,12},{12,14},{14,0},{1,3},{3,5},... | collective-permute-start | bytes 1048328 | tf_op jit(solution)/shard_map/ppermute | solution.py:30
  69.8 97.8 %collective-permute-start.7 = (bf16[520,2688]{1,0:T(8,128)(2,1)S(1)}, bf16[520,2688]{1,0:T(8,128)(2,1)}, u32[]{:S(2)}, u32[]{:S(2)}) collective-permute-start(bf16[520,2688]{1,0:T(8,128)(2,1)S(1)} %constant_dynamic-slice_fusion), channel_id=1, source_target_pairs={{0,1},{1,0},{2,3},{3,2},{4,5},{5,4},{6,7},{7,6},{8,9},{9,8},{10,11... | collective-permute-start | bytes 8386568 | tf_op jit(solution)/shard_map/ppermute | solution.py:30
  172.7 2.4 copy-start
  175.1 124.0 %copy-start.3 = (f32[5376]{0:T(1024)}, f32[5376]{0:T(1024)S(1)}, u32[]{:S(2)}) copy-start(f32[5376]{0:T(1024)S(1)} %fusion.40) | copy-start | bytes 64516
  294.5 4.6 %slice-start = ((s8[5591040]{0:T(1024)(128)(4,1)}), s8[4194304]{0:T(1024)(128)(4,1)S(1)}, s32[]{:S(2)}) async-start(s8[5591040]{0:T(1024)(128)(4,1)} %bitcast.63), calls=%async_computation.2 | async-start | bytes 8388608
  297.6 1.5 slice-start.1
  299.2 2.1 copy-start.5
  302.0 15.1 %collective-permute-start.8 = (bf16[512,2,128]{0,2,1:T(8,128)(2,1)S(1)}, bf16[512,2,128]{0,2,1:T(8,128)(2,1)}, u32[]{:S(2)}, u32[]{:S(2)}) collective-permute-start(bf16[512,2,128]{0,2,1:T(8,128)(2,1)S(1)} %pad_maximum_fusion), channel_id=1, source_target_pairs={{0,32},{16,48},{32,64},{48,80},{64,96},{80,112},{96,128},{112,144}... | collective-permute-start | bytes 786440 | tf_op jit(solution)/shard_map/ppermute | solution.py:19
  306.0 11.1 %collective-permute-start.9 = (bf16[512,2,128]{0,2,1:T(8,128)(2,1)S(1)}, bf16[512,2,128]{0,2,1:T(8,128)(2,1)}, u32[]{:S(2)}, u32[]{:S(2)}) collective-permute-start(bf16[512,2,128]{0,2,1:T(8,128)(2,1)S(1)} %pad_maximum_fusion), channel_id=1, source_target_pairs={{0,16},{16,32},{32,48},{48,64},{64,80},{80,96},{96,112},{112,128},... | collective-permute-start | bytes 786440 | tf_op jit(solution)/shard_map/ppermute | solution.py:19
  311.6 5.2 %copy-start.6 = (f32[128]{0:T(128)S(1)}, f32[128]{0:T(128)}, u32[]{:S(2)}) copy-start(f32[128]{0:T(128)} %param.9) | copy-start | bytes 1540
  311.6 6.5 %copy-start.1 = (pred[512,1536]{0,1:T(8,128)(4,1)S(1)}, pred[512,1536]{0,1:T(8,128)(4,1)}, u32[]{:S(2)}) copy-start(pred[512,1536]{0,1:T(8,128)(4,1)} %fusion.16) | copy-start | bytes 2359300
Sparse Core Ops, SparseCore 0:
  13.3 150.4 all-reduce.2
  166.2 127.2 all-reduce.4
